TPU v7x, 32 devices: a whole 2x2x4 slice. The times are simulated.
32 devices in a mesh: stream: 2 (over y), dev: 16 (over z, x, core).
Axes of the slice: x: 2, y: 2, z: 4, core: 2. Of those that a mesh axis runs over, the one named last changes fastest.
Arguments:
- latents: bfloat16 [32, 2, 3, 16, 1664], P(('stream', 'dev')), parts along dimension 0, may hold values from -6 to 6
- owners: int32 [4], P('stream'), parts along dimension 0, may hold values from 0 to 15
- conv_in: bfloat16 [432, 384], replicated, may hold values from -0.3125 to 0.3125
- conv_mid: bfloat16 [10368, 384], replicated, may hold values from -0.0625 to 0.0625
- to_pixels: bfloat16 [384, 12], replicated, may hold values from -0.3125 to 0.3125
Outputs:
- pixels: bfloat16 [4, 3, 32, 624], P('stream', None, 'dev'), parts along dimension 0
There are 2 independent parts, one for each index of `stream`. A program takes and returns all parts, laid end to end along the dimension named above; an argument that names none is the same for every part. Nothing has to cross between parts.
Inputs may be any that keep to these rules, and one draw needn't show every extreme that they name: `owners`: each entry is the index of a device on dev.
All inputs are finite; a program needn't handle non-finite values.
Results may differ from a plain program's by a relative error of at most 0.0052.
Values may be sent and summed in bfloat16 or wider, within the bound.
No kernel may reach another device: no remote copies, remote signals or barrier semaphores. Data moves between devices by JAX's collectives and lax.ppermute only.
A program may use at most 128 MiB of HBM per device.

v0:
```python
import jax
import jax.numpy as jnp
from jax import lax
from jax.sharding import PartitionSpec as P

ZC = 16
GROUPS = 2
FRAMES = 3
epsilon = 1e-06


def spread(value, axis, source):
    kept = jnp.where(lax.axis_index(axis) == source, value, 0).astype(value.dtype)
    return lax.psum(kept, axis)


def with_halo(block, sides, width):
    for axis, dim in sides:
        count = lax.axis_size(axis)
        forward = [(i, i + 1) for i in range(count - 1)]
        backward = [(target, source) for source, target in forward]
        low = lax.ppermute(
            lax.slice_in_dim(block, block.shape[dim] - width, None, axis=dim), axis, forward
        )
        high = lax.ppermute(lax.slice_in_dim(block, 0, width, axis=dim), axis, backward)
        block = jnp.concatenate([low, block, high], axis=dim)
    return block


def local_conv(source, weights):
    steps_t = source.shape[0] - 2
    rows_out = source.shape[1] - 2
    columns = source.shape[2]
    channels = source.shape[3]
    padded = jnp.pad(source, ((0, 0), (0, 0), (1, 1), (0, 0)))
    result = jnp.zeros((steps_t * rows_out * columns, weights.shape[1]), jnp.float32)
    for step_t in range(3):
        pieces = []
        for step_r in range(3):
            for step_w in range(3):
                pieces.append(
                    padded[
                        step_t : step_t + steps_t,
                        step_r : step_r + rows_out,
                        step_w : step_w + columns,
                    ]
                )
        stacked = jnp.concatenate(pieces, axis=-1)
        block = weights[step_t * 9 * channels : (step_t + 1) * 9 * channels]
        result = result + jnp.dot(
            stacked.reshape(-1, stacked.shape[-1]), block, preferred_element_type=jnp.float32
        )
    return result.reshape(steps_t, rows_out, columns, weights.shape[1])


def rms_scale(values):
    return values * lax.rsqrt(jnp.mean(values * values, axis=-1, keepdims=True) + epsilon)


def local(latents, owners, conv_in, conv_mid, to_pixels):
    n_devices = lax.axis_size("dev")
    position = lax.axis_index("dev")
    height = latents.shape[3]
    rows_dev = height // n_devices
    columns = latents.shape[4] // ZC
    channels = conv_mid.shape[1]
    first_row = position * rows_dev
    extend = 0
    span_rows = rows_dev + 2 * extend
    latent_cache = jnp.zeros((2, height + 4, columns, ZC), jnp.bfloat16)
    middle_cache = jnp.zeros((2, rows_dev + 2, columns, channels), jnp.bfloat16)
    results = []
    for group in range(GROUPS):
        group_latent = spread(latents[0, group], "dev", owners[group])
        frames = group_latent.reshape(FRAMES, height, columns, ZC)
        frames = jnp.pad(frames, ((0, 0), (2, 2), (0, 0), (0, 0)))
        history = jnp.concatenate([latent_cache, frames], axis=0)
        latent_cache = history[-2:]
        window = lax.dynamic_slice_in_dim(history, first_row + 1 - extend, span_rows + 2, 1)
        first_act = local_conv(window, conv_in)
        activated = jax.nn.silu(rms_scale(first_act)).astype(jnp.bfloat16)
        extended = with_halo(activated, (("dev", 1),), 1)
        middle_history = jnp.concatenate([middle_cache, extended], axis=0)
        middle_cache = middle_history[-2:]
        second_act = local_conv(middle_history, conv_mid)
        normed = rms_scale(first_act + second_act).astype(jnp.bfloat16)
        projected = jnp.dot(
            normed.reshape(-1, channels), to_pixels, preferred_element_type=jnp.float32
        )
        projected = projected.reshape(FRAMES, rows_dev, columns, 2, 2, 3).transpose(
            0, 1, 3, 2, 4, 5
        )
        results.append(projected.reshape(FRAMES, 2 * rows_dev, 6 * columns).astype(jnp.bfloat16))
    return jnp.stack(results, axis=0)


def solution(mesh):
    in_specs = (P(("stream", "dev"), None, None, None, None), P("stream"), P(), P(), P())
    out_specs = P("stream", None, "dev", None)
    return jax.shard_map(local, mesh=mesh, in_specs=in_specs, out_specs=out_specs, check_vma=False)
```

profile of v0, /device:TPU:3, one launch (start us, length us, event | category | flops | bytes accessed | tf_op | source)
XLA Modules:
  0.0 174.3 jit_solution(17543781535209339910)
XLA Ops:
  6.5 1.3 fusion.50
  9.2 1.0 slice_select_fusion
  10.2 2.0 %reshape.290 = bf16[3,16,104,16]{3,2,1,0:T(8,128)(2,1)} reshape(bf16[1,1,3,16,1664]{4,3,2,1,0:T(8,128)(2,1)S(1)} %get-tuple-element.59) | data formatting | bytes 319488 | tf_op jit(solution)/shard_map/reshape | solution.py:75
  12.2 2.0 %reshape.298 = bf16[3,16,104,16]{3,2,1,0:T(8,128)(2,1)} reshape(bf16[1,1,3,16,1664]{4,3,2,1,0:T(8,128)(2,1)S(1)} %get-tuple-element.58) | data formatting | bytes 319488 | tf_op jit(solution)/shard_map/reshape | solution.py:75
  14.2 99.9 %all-reduce.11.cloned.1.call-done = (bf16[3,16,104,16]{3,2,1,0:T(8,128)(2,1)}, bf16[3,16,104,16]{3,2,1,0:T(8,128)(2,1)}) async-done(((bf16[3,16,104,16]{3,2,1,0:T(8,128)(2,1)}, bf16[3,16,104,16]{3,2,1,0:T(8,128)(2,1)}), (bf16[3,16,104,16]{3,2,1,0:T(8,128)(2,1)}, bf16[3,16,104,16]{3,2,1,0:T(8,128)(2,1)})) %all-reduce.11.cloned.1.call-update) | async-done | bytes 319504 | tf_op jit(solution)/shard_map/psum | solution.py:14
  114.1 1.6 pad.23
  116.3 0.3 concatenate.89
  116.6 0.4 copy-done.2
  116.9 0.2 fusion.47
  117.1 0.3 concatenate.90
  117.4 0.2 convolution_add_fusion.3
  117.7 0.3 concatenate.91
  118.0 0.3 multiply_reduce_fusion.3
  118.4 0.2 multiply_convert_fusion.5
  118.6 5.2 %collective-permute-start = (bf16[3,1,104,384]{3,2,0,1:T(8,128)(2,1)S(1)}, bf16[3,1,104,384]{3,2,0,1:T(8,128)(2,1)}, u32[]{:S(2)}, u32[]{:S(2)}) collective-permute-start(bf16[3,1,104,384]{3,2,0,1:T(8,128)(2,1)S(1)} %multiply_convert_fusion.5), channel_id=1, source_target_pairs={{0,1},{1,2},{2,3},{3,4},{4,5},{5,6},{6,7},{7,8},{8,9},{9,10},{10,1... | collective-permute-start | bytes 718856 | tf_op jit(solution)/shard_map/ppermute | solution.py:22
  123.8 1.9 %collective-permute-start.1 = (bf16[3,1,104,384]{3,2,0,1:T(8,128)(2,1)S(1)}, bf16[3,1,104,384]{3,2,0,1:T(8,128)(2,1)}, u32[]{:S(2)}, u32[]{:S(2)}) collective-permute-start(bf16[3,1,104,384]{3,2,0,1:T(8,128)(2,1)S(1)} %multiply_convert_fusion.5), channel_id=1, source_target_pairs={{1,0},{2,1},{3,2},{4,3},{5,4},{6,5},{7,6},{8,7},{9,8},{10,9},{11,1... | collective-permute-start | bytes 718856 | tf_op jit(solution)/shard_map/ppermute | solution.py:25
  126.0 0.3 copy.13
  126.3 1.7 copy.21
  129.5 0.3 fusion.45
  130.2 0.3 convolution_add_fusion.1
  130.5 0.4 multiply_reduce_fusion.1
  131.0 0.2 multiply_convert_fusion.2
  131.2 4.5 %collective-permute-start.2 = (bf16[3,1,104,384]{3,2,0,1:T(8,128)(2,1)S(1)}, bf16[3,1,104,384]{3,2,0,1:T(8,128)(2,1)S(1)}, u32[]{:S(2)}, u32[]{:S(2)}) collective-permute-start(bf16[3,1,104,384]{3,2,0,1:T(8,128)(2,1)S(1)} %multiply_convert_fusion.2), channel_id=1, source_target_pairs={{0,1},{1,2},{2,3},{3,4},{4,5},{5,6},{6,7},{7,8},{8,9},{9,10},{10,1... | collective-permute-start | bytes 718856 | tf_op jit(solution)/shard_map/ppermute | solution.py:22
  135.8 2.1 %collective-permute-start.3 = (bf16[3,1,104,384]{3,2,0,1:T(8,128)(2,1)S(1)}, bf16[3,1,104,384]{3,2,0,1:T(8,128)(2,1)S(1)}, u32[]{:S(2)}, u32[]{:S(2)}) collective-permute-start(bf16[3,1,104,384]{3,2,0,1:T(8,128)(2,1)S(1)} %multiply_convert_fusion.2), channel_id=1, source_target_pairs={{1,0},{2,1},{3,2},{4,3},{5,4},{6,5},{7,6},{8,7},{9,8},{10,9},{11,1... | collective-permute-start | bytes 718856 | tf_op jit(solution)/shard_map/ppermute | solution.py:25
  137.9 1.2 pad_maximum_fusion
  139.3 0.4 pad_slice_fusion.31
  140.6 1.0 constant_dynamic-update-slice_fusion.6
  141.7 0.2 fusion.32
  142.0 2.2 %collective-permute-done.3 = bf16[3,1,104,384]{3,2,0,1:T(8,128)(2,1)S(1)} collective-permute-done((bf16[3,1,104,384]{3,2,0,1:T(8,128)(2,1)S(1)}, bf16[3,1,104,384]{3,2,0,1:T(8,128)(2,1)S(1)}, u32[]{:S(2)}, u32[]{:S(2)}) %collective-permute-start.3) | collective-permute-done | bytes 239648 | tf_op jit(solution)/shard_map/ppermute | solution.py:25
  144.4 0.4 pad_slice_fusion.25
  145.7 1.1 copy-done.5
  146.9 1.8 %constant_dynamic-update-slice_fusion.1 = bf16[312,3456]{1,0:T(8,128)(2,1)S(1)} fusion(bf16[312,3456]{1,0:T(8,128)(2,1)S(1)} %constant_dynamic-update-slice_fusion.2, bf16[312,384]{1,0:T(8,128)(2,1)} %bitcast.13), kind=kLoop, calls=%fused_computation.95 | loop fusion | bytes 479232
  148.9 0.3 slice-done.2
  149.2 1.3 fusion.6
  150.5 1.4 fusion.12
  151.9 1.5 multiply_reduce_fusion.2
  153.5 0.2 fusion.30
  153.8 0.3 copy.12
  154.0 0.4 convert_element_type.96
  154.6 0.2 fusion.33
  154.8 1.2 copy-done.4
  156.0 3.2 %fusion.4 = f32[312,384]{1,0:T(8,128)S(1)} fusion(bf16[312,3456]{1,0:T(8,128)(2,1)S(1)} %bitcast.98, bf16[10368,384]{1,0:T(8,128)(2,1)} %param.8), kind=kOutput, calls=%fused_computation.14 | convolution fusion | flops 828112896 | bytes 5289984 | tf_op jit(solution)/shard_map/dot_general | solution.py:50
  159.4 3.1 %fusion.15 = f32[312,384]{1,0:T(8,128)S(1)} fusion(f32[312,384]{1,0:T(8,128)S(1)} %fusion.4, bf16[312,3456]{1,0:T(8,128)(2,1)S(1)} %bitcast.100, bf16[10368,384]{1,0:T(8,128)(2,1)} %param.8), kind=kOutput, calls=%fused_computation.28 | convolution fusion | flops 828232704 | bytes 5769216 | tf_op jit(solution)/shard_map/dot_general | solution.py:50
  162.6 3.2 %multiply_reduce_fusion = (f32[312]{0:T(512)S(1)}, f32[312,384]{1,0:T(8,128)S(1)}) fusion(f32[312,384]{1,0:T(8,128)S(1)} %get-tuple-element.72, f32[312,384]{1,0:T(8,128)S(1)} %fusion.15, bf16[312,3456]{1,0:T(8,128)(2,1)S(1)} %constant_dynamic-update-slice_fusion.35, bf16[10368,384]{1,0:T(8,128)(2,1)} %param.8), kind=kOutput, calls=%fused_computation.45 | convolution fusion | flops 828591808 | bytes 6249696 | tf_op jit(solution)/shard_map/dot_general | solution.py:50
  165.9 0.2 fusion.31
  166.1 0.3 copy.18
  166.4 0.4 convert_element_type.103
  166.8 0.6 pad_maximum_fusion.1
  (110 shorter events, 5.9 us)
Async XLA Ops:
  6.5 107.6 %all-reduce.11.cloned.1.call-start = ((), (), s32[]{:S(2)}) async-start(), calls=%async_computation | async-start | bytes 5111808 | tf_op jit(solution)/shard_map/psum | solution.py:14
  12.2 2.0 %copy-start.7 = (bf16[384,12]{0,1:T(8,128)(2,1)S(1)}, bf16[384,12]{0,1:T(8,128)(2,1)}, u32[]{:S(2)}) copy-start(bf16[384,12]{0,1:T(8,128)(2,1)} %param.9) | copy-start | bytes 27652
  115.9 1.0 copy-start.2
  117.4 8.3 %copy-start.1 = (bf16[3,16,104,16]{3,2,1,0:T(8,128)(2,1)S(1)}, bf16[3,16,104,16]{3,2,1,0:T(8,128)(2,1)}, u32[]{:S(2)}) copy-start(bf16[3,16,104,16]{3,2,1,0:T(8,128)(2,1)} %get-tuple-element.5) | copy-start | bytes 479236
  118.6 19.3 %collective-permute-start = (bf16[3,1,104,384]{3,2,0,1:T(8,128)(2,1)S(1)}, bf16[3,1,104,384]{3,2,0,1:T(8,128)(2,1)}, u32[]{:S(2)}, u32[]{:S(2)}) collective-permute-start(bf16[3,1,104,384]{3,2,0,1:T(8,128)(2,1)S(1)} %multiply_convert_fusion.5), channel_id=1, source_target_pairs={{0,1},{1,2},{2,3},{3,4},{4,5},{5,6},{6,7},{7,8},{8,9},{9,10},{10,1... | collective-permute-start | bytes 718856 | tf_op jit(solution)/shard_map/ppermute | solution.py:22
  123.8 14.1 %collective-permute-start.1 = (bf16[3,1,104,384]{3,2,0,1:T(8,128)(2,1)S(1)}, bf16[3,1,104,384]{3,2,0,1:T(8,128)(2,1)}, u32[]{:S(2)}, u32[]{:S(2)}) collective-permute-start(bf16[3,1,104,384]{3,2,0,1:T(8,128)(2,1)S(1)} %multiply_convert_fusion.5), channel_id=1, source_target_pairs={{1,0},{2,1},{3,2},{4,3},{5,4},{6,5},{7,6},{8,7},{9,8},{10,9},{11,1... | collective-permute-start | bytes 718856 | tf_op jit(solution)/shard_map/ppermute | solution.py:25
  131.2 10.7 %collective-permute-start.2 = (bf16[3,1,104,384]{3,2,0,1:T(8,128)(2,1)S(1)}, bf16[3,1,104,384]{3,2,0,1:T(8,128)(2,1)S(1)}, u32[]{:S(2)}, u32[]{:S(2)}) collective-permute-start(bf16[3,1,104,384]{3,2,0,1:T(8,128)(2,1)S(1)} %multiply_convert_fusion.2), channel_id=1, source_target_pairs={{0,1},{1,2},{2,3},{3,4},{4,5},{5,6},{6,7},{7,8},{8,9},{9,10},{10,1... | collective-permute-start | bytes 718856 | tf_op jit(solution)/shard_map/ppermute | solution.py:22
  135.8 8.3 %collective-permute-start.3 = (bf16[3,1,104,384]{3,2,0,1:T(8,128)(2,1)S(1)}, bf16[3,1,104,384]{3,2,0,1:T(8,128)(2,1)S(1)}, u32[]{:S(2)}, u32[]{:S(2)}) collective-permute-start(bf16[3,1,104,384]{3,2,0,1:T(8,128)(2,1)S(1)} %multiply_convert_fusion.2), channel_id=1, source_target_pairs={{1,0},{2,1},{3,2},{4,3},{5,4},{6,5},{7,6},{8,7},{9,8},{10,9},{11,1... | collective-permute-start | bytes 718856 | tf_op jit(solution)/shard_map/ppermute | solution.py:25
  139.1 1.4 copy-start
  140.6 3.6 %slice-start = ((bf16[3,3,104,384]{3,2,0,1:T(8,128)(2,1)}), bf16[2,3,104,384]{3,2,0,1:T(8,128)(2,1)S(1)}, s32[]{:S(2)}) async-start(bf16[3,3,104,384]{3,2,0,1:T(8,128)(2,1)} %copy-done), calls=%async_computation.1 | async-start | bytes 958464 | tf_op jit(solution)/shard_map/slice | solution.py:84
  145.0 3.9 %slice-start.1 = ((s8[7962624]{0:T(1024)(128)(4,1)}), s8[4194304]{0:T(1024)(128)(4,1)S(1)}, s32[]{:S(2)}) async-start(s8[7962624]{0:T(1024)(128)(4,1)} %bitcast.102), calls=%async_computation.2 | async-start | bytes 8388608
  145.4 1.4 copy-start.5
  145.5 3.7 %slice-start.2 = ((s8[7962624]{0:T(1024)(128)(4,1)}), s8[3768320]{0:T(1024)(128)(4,1)S(1)}, s32[]{:S(2)}) async-start(s8[7962624]{0:T(1024)(128)(4,1)} %bitcast.102), calls=%async_computation.3 | async-start | bytes 7536640
  148.9 1.7 copy-start.3
  154.4 1.6 copy-start.4
  156.0 3.4 %copy-start.6 = (bf16[3,1,104,3456]{3,2,0,1:T(8,128)(2,1)S(1)}, bf16[3,1,104,3456]{3,2,0,1:T(8,128)(2,1)}, u32[]{:S(2)}) copy-start(bf16[3,1,104,3456]{3,2,0,1:T(8,128)(2,1)} %copy-done.5) | copy-start | bytes 6469636
Sparse Core Ops, SparseCore 0:
  14.3 99.7 all-reduce.10
where the time goes:
time: 175 us; the launch traced here: 174 us
  waiting for transfers between devices  102 us (58%)
  local copies, waits for them, and re-layouts  22.8 us (13%)
  matrix products  15.9 us (9%)
  between operations  15.4 us (9%)
  starting transfers between devices  13.8 us (8%)
  other arithmetic  4.23 us (2%)
    psum x1, waiting for transfers between devices, spread(): return lax.psum(kept, axis)  99.9 us
    dot_general x12, matrix products, local_conv(): jnp.dot(stacked.reshape(-1, stacked.shape[-1]), block, preferred_element_...  15.5 us
    unnamed x78, local copies, waits for them, and re-layouts  10.4 us
    ppermute x2, starting transfers between devices, with_halo(): lax.ppermute(lax.slice_in_dim(block, block.shape[dim] - width, None, axis...  9.76 us
    ppermute x2, starting transfers between devices, with_halo(): lax.ppermute(lax.slice_in_dim(block, 0, width, axis=dim), axis, backward)  4.02 us
    reshape x2, local copies, waits for them, and re-layouts, local(): frames = group_latent.reshape(FRAMES, height, columns, ZC)  3.94 us
  transfers between devices with their start and end apart: 5, of which 2 were waited for; matrix products, arithmetic and copies ran while one was open for 5% of the time, Pallas kernels for 0%

commit v1 on v0

--- a/solution.py
+++ b/solution.py
@@ -2,6 +2,7 @@
 import jax.numpy as jnp
 from jax import lax
 from jax.sharding import PartitionSpec as P
+from jax.lax import all_gather
 
 ZC = 16
 GROUPS = 2
@@ -11,7 +12,11 @@
 
 def spread(value, axis, source):
     kept = jnp.where(lax.axis_index(axis) == source, value, 0).astype(value.dtype)
-    return lax.psum(kept, axis)
+
+    def raise_region_now(row_data, dev_axis):
+        return all_gather(row_data, dev_axis).sum(axis=0)
+
+    return raise_region_now(kept, axis)
 
 
 def with_halo(block, sides, width):

time: 175 us -> 149 us (0.85)
  waiting for transfers between devices: 102 us -> 73 us
  other arithmetic: 4.23 us -> 9.2 us
  starting transfers between devices: 13.8 us -> 11.9 us
    psum x1 -> x0, waiting for transfers between devices: 99.9 us -> none  [spread(): return lax.psum(kept, axis)]
    all_gather x0 -> x2, waiting for transfers between devices: none -> 70.1 us  [raise_region_now(): return all_gather(row_data, dev_axis).sum(axis=0)]
    reduce_sum x0 -> x2, other arithmetic: none -> 4.23 us  [raise_region_now(): return all_gather(row_data, dev_axis).sum(axis=0)]
    reshape x2, local copies, waits for them, and re-layouts: 3.94 us -> 1.84 us  [local(): frames = group_latent.reshape(FRAMES, height, columns, ZC)]
    concatenate x14, local copies, waits for them, and re-layouts: 1.81 us -> 3.82 us  [local_conv(): stacked = jnp.concatenate(pieces, axis=-1)]
    ppermute x2, starting transfers between devices: 9.76 us -> 7.81 us  [with_halo(): lax.ppermute(lax.slice_in_dim(block, block.shape[dim] - width, None, axis...]
    unnamed x78 -> x76, local copies, waits for them, and re-layouts: 10.4 us -> 8.69 us
  transfers between devices with their start and end apart: 5 -> 6, of which waited for: 2 -> 3; matrix products, arithmetic and copies ran while one was open for 5% -> 15% of each run, Pallas kernels for 0% -> 0%
where the time goes in v1:
time: 149 us; the launch traced here: 148 us
  waiting for transfers between devices  73 us (49%)
  local copies, waits for them, and re-layouts  22.5 us (15%)
  matrix products  15.9 us (11%)
  between operations  15.4 us (10%)
  starting transfers between devices  11.9 us (8%)
  other arithmetic  9.2 us (6%)
    all_gather x2, waiting for transfers between devices, raise_region_now(): return all_gather(row_data, dev_axis).sum(axis=0)  70.1 us
    dot_general x12, matrix products, local_conv(): jnp.dot(stacked.reshape(-1, stacked.shape[-1]), block, preferred_element_...  15.5 us
    unnamed x76, local copies, waits for them, and re-layouts  8.69 us
    ppermute x2, starting transfers between devices, with_halo(): lax.ppermute(lax.slice_in_dim(block, block.shape[dim] - width, None, axis...  7.81 us
    reduce_sum x2, other arithmetic, raise_region_now(): return all_gather(row_data, dev_axis).sum(axis=0)  4.23 us
    ppermute x2, starting transfers between devices, with_halo(): lax.ppermute(lax.slice_in_dim(block, 0, width, axis=dim), axis, backward)  4.02 us
    concatenate x14, local copies, waits for them, and re-layouts, local_conv(): stacked = jnp.concatenate(pieces, axis=-1)  3.82 us
  transfers between devices with their start and end apart: 6, of which 3 were waited for; matrix products, arithmetic and copies ran while one was open for 15% of the time, Pallas kernels for 0%

profile of v1, /device:TPU:3, one launch (start us, length us, event | category | flops | bytes accessed | tf_op | source)
XLA Modules:
  0.0 148.0 jit_solution(14721160151168851271)
XLA Ops:
  6.5 1.3 fusion.50
  9.2 1.8 %slice_select_fusion = (bf16[1,1,3,16,1664]{4,3,2,1,0:T(8,128)(2,1)}, bf16[1,1,3,16,1664]{4,3,2,1,0:T(8,128)(2,1)}) fusion(bf16[1,2,3,16,1664]{4,3,2,1,0:T(8,128)(2,1)} %param.5, pred[]{:T(512)S(6)} %eq.7, pred[]{:T(512)S(6)} %eq.6), kind=kLoop, calls=%fused_computation.137 | loop fusion | flops 159744 | bytes 638978 | tf_op jit(solution)/shard_map/jit(_where)/select_n | solution.py:14
  11.1 0.7 all-gather.7.cloned.1.call-update
  11.8 0.7 reshape.329
  12.5 42.4 %all-gather.5.cloned.1.call-done = bf16[16,1,3,16,1664]{4,3,2,1,0:T(8,128)(2,1)} async-done(((bf16[1,1,3,16,1664]{4,3,2,1,0:T(8,128)(2,1)}), bf16[16,1,3,16,1664]{4,3,2,1,0:T(8,128)(2,1)}) %all-gather.5.cloned.1.call-update) | async-done | bytes 2555920 | tf_op jit(solution)/shard_map/all_gather | solution.py:17
  54.9 2.1 %reduce_sum.60 = bf16[3,16,1664]{2,1,0:T(8,128)(2,1)S(1)} reduce(bf16[16,1,3,16,1664]{4,3,2,1,0:T(8,128)(2,1)} %all-gather.5.cloned.1.call-done, bf16[]{:T(256)} %constant.23.clone.1), dimensions={0,1}, to_apply=%region_0.1 | reduce | flops 1198080 | bytes 2715650 | tf_op jit(solution)/shard_map/reduce_sum | solution.py:17
  57.0 0.9 reshape.310
  57.9 0.3 pad.23
  58.5 0.9 pad_slice_fusion.8
  59.4 0.9 pad_dynamic-slice_fusion
  60.2 1.4 concatenate.91
  61.6 1.2 concatenate.90
  62.8 0.3 concatenate.89
  63.3 0.2 convolution_add_fusion.3
  63.6 0.3 multiply_reduce_fusion.3
  64.2 3.9 %collective-permute-start = (bf16[3,1,104,384]{3,2,0,1:T(8,128)(2,1)S(1)}, bf16[3,1,104,384]{3,2,0,1:T(8,128)(2,1)}, u32[]{:S(2)}, u32[]{:S(2)}) collective-permute-start(bf16[3,1,104,384]{3,2,0,1:T(8,128)(2,1)S(1)} %multiply_convert_fusion.5), channel_id=1, source_target_pairs={{0,1},{1,2},{2,3},{3,4},{4,5},{5,6},{6,7},{7,8},{8,9},{9,10},{10,1... | collective-permute-start | bytes 718856 | tf_op jit(solution)/shard_map/ppermute | solution.py:27
  68.1 1.9 %collective-permute-start.1 = (bf16[3,1,104,384]{3,2,0,1:T(8,128)(2,1)S(1)}, bf16[3,1,104,384]{3,2,0,1:T(8,128)(2,1)}, u32[]{:S(2)}, u32[]{:S(2)}) collective-permute-start(bf16[3,1,104,384]{3,2,0,1:T(8,128)(2,1)S(1)} %multiply_convert_fusion.5), channel_id=1, source_target_pairs={{1,0},{2,1},{3,2},{4,3},{5,4},{6,5},{7,6},{8,7},{9,8},{10,9},{11,1... | collective-permute-start | bytes 718856 | tf_op jit(solution)/shard_map/ppermute | solution.py:30
  70.2 1.0 copy.13
  71.2 27.7 %all-gather.7.cloned.1.call-done = bf16[16,1,3,16,1664]{4,3,2,1,0:T(8,128)(2,1)} async-done(((bf16[1,1,3,16,1664]{4,3,2,1,0:T(8,128)(2,1)}), bf16[16,1,3,16,1664]{4,3,2,1,0:T(8,128)(2,1)}) %all-gather.7.cloned.1.call-update) | async-done | bytes 2555920 | tf_op jit(solution)/shard_map/all_gather | solution.py:17
  98.9 2.1 %reduce_sum.63 = bf16[3,16,1664]{2,1,0:T(8,128)(2,1)S(1)} reduce(bf16[16,1,3,16,1664]{4,3,2,1,0:T(8,128)(2,1)} %all-gather.7.cloned.1.call-done, bf16[]{:T(256)} %constant.23.clone.1), dimensions={0,1}, to_apply=%region_3.4 | reduce | flops 1198080 | bytes 2715650 | tf_op jit(solution)/shard_map/reduce_sum | solution.py:17
  101.1 0.9 reshape.318
  102.0 0.4 copy.21
  103.9 0.3 fusion.45
  104.6 0.3 convolution_add_fusion.1
  104.9 0.4 multiply_reduce_fusion.1
  105.6 3.9 %collective-permute-start.2 = (bf16[3,1,104,384]{3,2,0,1:T(8,128)(2,1)S(1)}, bf16[3,1,104,384]{3,2,0,1:T(8,128)(2,1)S(1)}, u32[]{:S(2)}, u32[]{:S(2)}) collective-permute-start(bf16[3,1,104,384]{3,2,0,1:T(8,128)(2,1)S(1)} %multiply_convert_fusion.2), channel_id=1, source_target_pairs={{0,1},{1,2},{2,3},{3,4},{4,5},{5,6},{6,7},{7,8},{8,9},{9,10},{10,1... | collective-permute-start | bytes 718856 | tf_op jit(solution)/shard_map/ppermute | solution.py:27
  109.5 2.1 %collective-permute-start.3 = (bf16[3,1,104,384]{3,2,0,1:T(8,128)(2,1)S(1)}, bf16[3,1,104,384]{3,2,0,1:T(8,128)(2,1)S(1)}, u32[]{:S(2)}, u32[]{:S(2)}) collective-permute-start(bf16[3,1,104,384]{3,2,0,1:T(8,128)(2,1)S(1)} %multiply_convert_fusion.2), channel_id=1, source_target_pairs={{1,0},{2,1},{3,2},{4,3},{5,4},{6,5},{7,6},{8,7},{9,8},{10,9},{11,1... | collective-permute-start | bytes 718856 | tf_op jit(solution)/shard_map/ppermute | solution.py:30
  111.6 1.2 pad_maximum_fusion
  113.0 0.4 pad_slice_fusion.31
  114.3 1.0 constant_dynamic-update-slice_fusion.6
  115.7 2.2 %collective-permute-done.3 = bf16[3,1,104,384]{3,2,0,1:T(8,128)(2,1)S(1)} collective-permute-done((bf16[3,1,104,384]{3,2,0,1:T(8,128)(2,1)S(1)}, bf16[3,1,104,384]{3,2,0,1:T(8,128)(2,1)S(1)}, u32[]{:S(2)}, u32[]{:S(2)}) %collective-permute-start.3) | collective-permute-done | bytes 239648 | tf_op jit(solution)/shard_map/ppermute | solution.py:30
  118.2 0.4 pad_slice_fusion.25
  119.4 1.1 copy-done.5
  120.6 1.8 %constant_dynamic-update-slice_fusion.1 = bf16[312,3456]{1,0:T(8,128)(2,1)S(1)} fusion(bf16[312,3456]{1,0:T(8,128)(2,1)S(1)} %constant_dynamic-update-slice_fusion.2, bf16[312,384]{1,0:T(8,128)(2,1)} %bitcast.13), kind=kLoop, calls=%fused_computation.95 | loop fusion | bytes 479232
  122.6 0.3 slice-done.2
  122.9 1.3 fusion.6
  124.3 1.4 fusion.12
  125.7 1.5 %multiply_reduce_fusion.2 = (f32[312]{0:T(512)S(1)}, f32[312,384]{1,0:T(8,128)S(1)}) fusion(f32[312,384]{1,0:T(8,128)S(1)} %get-tuple-element.72, f32[312,384]{1,0:T(8,128)S(1)} %fusion.12, bf16[312,3456]{1,0:T(8,128)(2,1)S(1)} %constant_dynamic-update-slice_fusion, bf16[10368,384]{1,0:T(8,128)(2,1)S(1)} %bitcast.99), kind=kOutput, calls=%fused_computation.50 | convolution fusion | flops 828591808 | bytes 6249696 | tf_op jit(solution)/shard_map/dot_general | solution.py:55
  127.5 0.3 copy.12
  127.7 0.4 convert_element_type.100
  128.3 0.2 fusion.33
  128.5 1.2 copy-done.4
  129.7 3.2 %fusion.4 = f32[312,384]{1,0:T(8,128)S(1)} fusion(bf16[312,3456]{1,0:T(8,128)(2,1)S(1)} %bitcast.94, bf16[10368,384]{1,0:T(8,128)(2,1)} %param.8), kind=kOutput, calls=%fused_computation.14 | convolution fusion | flops 828112896 | bytes 5289984 | tf_op jit(solution)/shard_map/dot_general | solution.py:55
  133.2 3.1 %fusion.15 = f32[312,384]{1,0:T(8,128)S(1)} fusion(f32[312,384]{1,0:T(8,128)S(1)} %fusion.4, bf16[312,3456]{1,0:T(8,128)(2,1)S(1)} %bitcast.96, bf16[10368,384]{1,0:T(8,128)(2,1)} %param.8), kind=kOutput, calls=%fused_computation.28 | convolution fusion | flops 828232704 | bytes 5769216 | tf_op jit(solution)/shard_map/dot_general | solution.py:55
  136.3 3.2 %multiply_reduce_fusion = (f32[312]{0:T(512)S(1)}, f32[312,384]{1,0:T(8,128)S(1)}) fusion(f32[312,384]{1,0:T(8,128)S(1)} %get-tuple-element.70, f32[312,384]{1,0:T(8,128)S(1)} %fusion.15, bf16[312,3456]{1,0:T(8,128)(2,1)S(1)} %constant_dynamic-update-slice_fusion.35, bf16[10368,384]{1,0:T(8,128)(2,1)} %param.8), kind=kOutput, calls=%fused_computation.45 | convolution fusion | flops 828591808 | bytes 6249696 | tf_op jit(solution)/shard_map/dot_general | solution.py:55
  139.9 0.3 copy.18
  140.1 0.4 convert_element_type.107
  140.5 0.6 pad_maximum_fusion.1
  (113 shorter events, 6.9 us)
Async XLA Ops:
  6.5 48.4 %all-gather.5.cloned.1.call-start = ((), (), s32[]{:S(2)}) async-start(), calls=%async_computation | async-start | bytes 2715648 | tf_op jit(solution)/shard_map/all_gather | solution.py:17
  11.0 87.9 %all-gather.7.cloned.1.call-start = ((), (), s32[]{:S(2)}) async-start(), calls=%async_computation.1 | async-start | bytes 2715648 | tf_op jit(solution)/shard_map/all_gather | solution.py:17
  59.4 3.7 %copy-start.1 = (bf16[432,384]{1,0:T(8,128)(2,1)S(1)}, bf16[432,384]{1,0:T(8,128)(2,1)}, u32[]{:S(2)}) copy-start(bf16[432,384]{1,0:T(8,128)(2,1)} %param.7) | copy-start | bytes 995332
  64.2 47.4 %collective-permute-start = (bf16[3,1,104,384]{3,2,0,1:T(8,128)(2,1)S(1)}, bf16[3,1,104,384]{3,2,0,1:T(8,128)(2,1)}, u32[]{:S(2)}, u32[]{:S(2)}) collective-permute-start(bf16[3,1,104,384]{3,2,0,1:T(8,128)(2,1)S(1)} %multiply_convert_fusion.5), channel_id=1, source_target_pairs={{0,1},{1,2},{2,3},{3,4},{4,5},{5,6},{6,7},{7,8},{8,9},{9,10},{10,1... | collective-permute-start | bytes 718856 | tf_op jit(solution)/shard_map/ppermute | solution.py:27
  68.1 43.5 %collective-permute-start.1 = (bf16[3,1,104,384]{3,2,0,1:T(8,128)(2,1)S(1)}, bf16[3,1,104,384]{3,2,0,1:T(8,128)(2,1)}, u32[]{:S(2)}, u32[]{:S(2)}) collective-permute-start(bf16[3,1,104,384]{3,2,0,1:T(8,128)(2,1)S(1)} %multiply_convert_fusion.5), channel_id=1, source_target_pairs={{1,0},{2,1},{3,2},{4,3},{5,4},{6,5},{7,6},{8,7},{9,8},{10,9},{11,1... | collective-permute-start | bytes 718856 | tf_op jit(solution)/shard_map/ppermute | solution.py:30
  71.2 31.2 %copy-start.2 = (bf16[2,20,104,16]{2,3,1,0:T(8,128)(2,1)S(1)}, bf16[2,20,104,16]{2,3,1,0:T(8,128)(2,1)}, u32[]{:S(2)}) copy-start(bf16[2,20,104,16]{2,3,1,0:T(8,128)(2,1)} %copy.13) | copy-start | bytes 399364
  105.6 10.1 %collective-permute-start.2 = (bf16[3,1,104,384]{3,2,0,1:T(8,128)(2,1)S(1)}, bf16[3,1,104,384]{3,2,0,1:T(8,128)(2,1)S(1)}, u32[]{:S(2)}, u32[]{:S(2)}) collective-permute-start(bf16[3,1,104,384]{3,2,0,1:T(8,128)(2,1)S(1)} %multiply_convert_fusion.2), channel_id=1, source_target_pairs={{0,1},{1,2},{2,3},{3,4},{4,5},{5,6},{6,7},{7,8},{8,9},{9,10},{10,1... | collective-permute-start | bytes 718856 | tf_op jit(solution)/shard_map/ppermute | solution.py:27
  109.5 8.3 %collective-permute-start.3 = (bf16[3,1,104,384]{3,2,0,1:T(8,128)(2,1)S(1)}, bf16[3,1,104,384]{3,2,0,1:T(8,128)(2,1)S(1)}, u32[]{:S(2)}, u32[]{:S(2)}) collective-permute-start(bf16[3,1,104,384]{3,2,0,1:T(8,128)(2,1)S(1)} %multiply_convert_fusion.2), channel_id=1, source_target_pairs={{1,0},{2,1},{3,2},{4,3},{5,4},{6,5},{7,6},{8,7},{9,8},{10,9},{11,1... | collective-permute-start | bytes 718856 | tf_op jit(solution)/shard_map/ppermute | solution.py:30
  112.8 1.4 copy-start
  114.3 3.6 %slice-start = ((bf16[3,3,104,384]{3,2,0,1:T(8,128)(2,1)}), bf16[2,3,104,384]{3,2,0,1:T(8,128)(2,1)S(1)}, s32[]{:S(2)}) async-start(bf16[3,3,104,384]{3,2,0,1:T(8,128)(2,1)} %copy-done), calls=%async_computation.2 | async-start | bytes 958464 | tf_op jit(solution)/shard_map/slice | solution.py:89
  118.7 3.9 %slice-start.1 = ((s8[7962624]{0:T(1024)(128)(4,1)}), s8[4194304]{0:T(1024)(128)(4,1)S(1)}, s32[]{:S(2)}) async-start(s8[7962624]{0:T(1024)(128)(4,1)} %bitcast.98), calls=%async_computation.3 | async-start | bytes 8388608
  119.1 1.4 copy-start.5
  119.3 3.7 %slice-start.2 = ((s8[7962624]{0:T(1024)(128)(4,1)}), s8[3768320]{0:T(1024)(128)(4,1)S(1)}, s32[]{:S(2)}) async-start(s8[7962624]{0:T(1024)(128)(4,1)} %bitcast.98), calls=%async_computation.4 | async-start | bytes 7536640
  122.6 1.7 %copy-start.3 = (bf16[3,1,104,3456]{3,2,0,1:T(8,128)(2,1)}, bf16[3,1,104,3456]{3,2,0,1:T(8,128)(2,1)S(1)}, u32[]{:S(2)}) copy-start(bf16[3,1,104,3456]{3,2,0,1:T(8,128)(2,1)S(1)} %get-tuple-element.77) | copy-start | bytes 6469636
  128.1 1.6 %copy-start.4 = (bf16[3,1,104,3456]{3,2,0,1:T(8,128)(2,1)S(1)}, bf16[3,1,104,3456]{3,2,0,1:T(8,128)(2,1)}, u32[]{:S(2)}) copy-start(bf16[3,1,104,3456]{3,2,0,1:T(8,128)(2,1)} %copy-done.3) | copy-start | bytes 6469636
  129.7 3.4 %copy-start.6 = (bf16[3,1,104,3456]{3,2,0,1:T(8,128)(2,1)S(1)}, bf16[3,1,104,3456]{3,2,0,1:T(8,128)(2,1)}, u32[]{:S(2)}) copy-start(bf16[3,1,104,3456]{3,2,0,1:T(8,128)(2,1)} %copy-done.5) | copy-start | bytes 6469636
Sparse Core Ops, SparseCore 0:
  11.1 43.7 all-gather.4
  57.1 41.8 all-gather.6
